TPU v7x, 512 devices: a whole 4x8x8 slice. The times are simulated.
512 devices in a mesh: section: 32 (over z, x), neuron: 16 (over y, core).
Axes of the slice: x: 4, y: 8, z: 8, core: 2. Of those that a mesh axis runs over, the one named last changes fastest.
Arguments:
- inputs: bfloat16 [6, 32768], P(None, 'neuron'), may hold values from 0 to 2
- weight_tiles: bfloat16 [32, 2048, 128, 128], P('section', 'neuron'), may hold values from -0.07324219 to 0.07910156
- source_block: int32 [32, 2048], P('section', 'neuron'), may hold values from 0 to 255
- target_block: int32 [32, 2048], P('section', 'neuron'), may hold values from 0 to 15
- live_slots: int32 [32, 16], P('section', 'neuron'), may hold values from 16 to 128, as said below
Outputs:
- activations: bfloat16 [32, 6, 32768], P('section', None, 'neuron')
Inputs may be any that keep to these rules, and one draw needn't show every extreme that they name: live_slots[l, n] is 128, 64, 32 or 16, and in every layer some shard has all 128 slots live.
All inputs are finite; a program needn't handle non-finite values.
Results may differ from a plain program's by a relative error of at most 0.0045.
Values may be sent and summed in bfloat16 or wider, within the bound.
No kernel may reach another device: no remote copies, remote signals or barrier semaphores. Data moves between devices by JAX's collectives and lax.ppermute only.
A program may use at most 64 MiB of HBM per device.

v0:
```python
import jax
import jax.numpy as jnp
from jax import lax
from jax.sharding import PartitionSpec as P

NEURON_BIAS = -0.3
CLIP_LEVEL = 32.0
UNROLL = True


def layer_apply(gathered, weight_tiles, source, selector):
    row_count = gathered.shape[0]
    block_size = weight_tiles.shape[2]
    column_count = selector.shape[1]
    block_count = gathered.shape[1] // block_size
    shaped = gathered.reshape(row_count, block_count, block_size)
    picked = shaped.at[:, source].get(mode="promise_in_bounds")
    partial_value = jnp.einsum(
        "msk,skj->msj", picked, weight_tiles[0], preferred_element_type=jnp.float32
    )
    summed = jnp.einsum("msj,sc->mcj", partial_value, selector, precision=lax.Precision.HIGHEST)
    result = jnp.clip(summed + NEURON_BIAS, 0.0, CLIP_LEVEL).astype(jnp.bfloat16)
    return result.reshape(row_count, column_count * block_size)


def local(inputs, weight_tiles, source_block, target_block, live_slots):
    section_pos = lax.axis_index("section")
    section_count = lax.axis_size("section")
    row_count, shard_width = inputs.shape
    slot_count = weight_tiles.shape[1]
    column_count = shard_width // weight_tiles.shape[2]
    source = source_block[0]
    live_mask = jnp.arange(slot_count, dtype=jnp.int32) < live_slots[0, 0]
    selector = (
        (target_block[0][:, None] == jnp.arange(column_count, dtype=jnp.int32)[None, :])
        & live_mask[:, None]
    ).astype(jnp.float32)

    def compute(gathered):
        return layer_apply(gathered, weight_tiles, source, selector)

    def empty(gathered):
        return jnp.zeros((row_count, shard_width), jnp.bfloat16)

    def step(step_num, current, collected, route):
        gathered = lax.all_gather(current, "neuron", axis=1, tiled=True)
        active = section_pos == step_num
        result = compute(gathered)
        collected = jnp.where(active, result, collected)
        if route is None:
            return (result, collected)
        return (lax.ppermute(result, "section", route), collected)

    collected = jnp.zeros((row_count, shard_width), jnp.bfloat16)
    current = inputs
    if UNROLL:
        for t in range(section_count - 1):
            current, collected = step(t, current, collected, [(t, t + 1)])
    else:
        route = [(i, i + 1) for i in range(section_count - 1)]
        current, collected = lax.fori_loop(
            0, section_count - 1, lambda t, c: step(t, c[0], c[1], route), (current, collected)
        )
    _, collected = step(section_count - 1, current, collected, None)
    return collected[None]


def solution(mesh):
    in_specs = (
        P(None, "neuron"),
        P("section", "neuron", None, None),
        P("section", "neuron"),
        P("section", "neuron"),
        P("section", "neuron"),
    )
    out_specs = P("section", None, "neuron")
    return jax.shard_map(local, mesh=mesh, in_specs=in_specs, out_specs=out_specs, check_vma=False)
```

profile of v0, /device:TPU:455, one launch (start us, length us, event | category | flops | bytes accessed | tf_op | source)
XLA Modules:
  0.0 809.9 jit_solution(16794483580277421957)
XLA Ops:
  0.7 19.8 %all_gather.96 = bf16[6,32768]{1,0:T(8,128)(2,1)S(1)} all-gather(bf16[6,2048]{1,0:T(8,128)(2,1)} %param.5), channel_id=1, replica_groups=mesh['section'=32,'neuron'=16] {'neuron'}, dimensions={1}, use_global_device_ids=true | all-gather | bytes 417792 | tf_op jit(solution)/shard_map/all_gather | solution.py:46
  47.7 16.8 %all_gather.98 = bf16[6,32768]{1,0:T(8,128)(2,1)S(1)} all-gather(bf16[6,2048]{1,0:T(8,128)(2,1)S(1)} %collective-permute-done.1), channel_id=1, replica_groups=mesh['section'=32,'neuron'=16] {'neuron'}, dimensions={1}, use_global_device_ids=true | all-gather | bytes 417792 | tf_op jit(solution)/shard_map/all_gather | solution.py:46
  91.2 16.8 %all_gather.100 = bf16[6,32768]{1,0:T(8,128)(2,1)S(1)} all-gather(bf16[6,2048]{1,0:T(8,128)(2,1)S(1)} %collective-permute-done.3), channel_id=1, replica_groups=mesh['section'=32,'neuron'=16] {'neuron'}, dimensions={1}, use_global_device_ids=true | all-gather | bytes 417792 | tf_op jit(solution)/shard_map/all_gather | solution.py:46
  134.7 16.8 %all_gather.102 = bf16[6,32768]{1,0:T(8,128)(2,1)S(1)} all-gather(bf16[6,2048]{1,0:T(8,128)(2,1)S(1)} %collective-permute-done.5), channel_id=1, replica_groups=mesh['section'=32,'neuron'=16] {'neuron'}, dimensions={1}, use_global_device_ids=true | all-gather | bytes 417792 | tf_op jit(solution)/shard_map/all_gather | solution.py:46
  178.2 17.2 %all_gather.104 = bf16[6,32768]{1,0:T(8,128)(2,1)S(1)} all-gather(bf16[6,2048]{1,0:T(8,128)(2,1)S(1)} %collective-permute-done.7), channel_id=1, replica_groups=mesh['section'=32,'neuron'=16] {'neuron'}, dimensions={1}, use_global_device_ids=true | all-gather | bytes 417792 | tf_op jit(solution)/shard_map/all_gather | solution.py:46
  222.2 16.8 %all_gather.106 = bf16[6,32768]{1,0:T(8,128)(2,1)S(1)} all-gather(bf16[6,2048]{1,0:T(8,128)(2,1)S(1)} %collective-permute-done.9), channel_id=1, replica_groups=mesh['section'=32,'neuron'=16] {'neuron'}, dimensions={1}, use_global_device_ids=true | all-gather | bytes 417792 | tf_op jit(solution)/shard_map/all_gather | solution.py:46
  265.7 16.8 %all_gather.108 = bf16[6,32768]{1,0:T(8,128)(2,1)S(1)} all-gather(bf16[6,2048]{1,0:T(8,128)(2,1)S(1)} %collective-permute-done.11), channel_id=1, replica_groups=mesh['section'=32,'neuron'=16] {'neuron'}, dimensions={1}, use_global_device_ids=true | all-gather | bytes 417792 | tf_op jit(solution)/shard_map/all_gather | solution.py:46
  309.2 16.7 %all_gather.110 = bf16[6,32768]{1,0:T(8,128)(2,1)S(1)} all-gather(bf16[6,2048]{1,0:T(8,128)(2,1)S(1)} %collective-permute-done.13), channel_id=1, replica_groups=mesh['section'=32,'neuron'=16] {'neuron'}, dimensions={1}, use_global_device_ids=true | all-gather | bytes 417792 | tf_op jit(solution)/shard_map/all_gather | solution.py:46
  352.6 16.9 %all_gather.112 = bf16[6,32768]{1,0:T(8,128)(2,1)S(1)} all-gather(bf16[6,2048]{1,0:T(8,128)(2,1)S(1)} %collective-permute-done.15), channel_id=1, replica_groups=mesh['section'=32,'neuron'=16] {'neuron'}, dimensions={1}, use_global_device_ids=true | all-gather | bytes 417792 | tf_op jit(solution)/shard_map/all_gather | solution.py:46
  396.1 16.7 %all_gather.114 = bf16[6,32768]{1,0:T(8,128)(2,1)S(1)} all-gather(bf16[6,2048]{1,0:T(8,128)(2,1)S(1)} %collective-permute-done.17), channel_id=1, replica_groups=mesh['section'=32,'neuron'=16] {'neuron'}, dimensions={1}, use_global_device_ids=true | all-gather | bytes 417792 | tf_op jit(solution)/shard_map/all_gather | solution.py:46
  417.9 16.4 %all_gather.115 = bf16[6,32768]{1,0:T(8,128)(2,1)S(1)} all-gather(bf16[6,2048]{1,0:T(8,128)(2,1)S(1)} %collective-permute-done.18), channel_id=1, replica_groups=mesh['section'=32,'neuron'=16] {'neuron'}, dimensions={1}, use_global_device_ids=true | all-gather | bytes 417792 | tf_op jit(solution)/shard_map/all_gather | solution.py:46
  439.3 16.7 %all_gather.116 = bf16[6,32768]{1,0:T(8,128)(2,1)S(1)} all-gather(bf16[6,2048]{1,0:T(8,128)(2,1)S(1)} %collective-permute-done.19), channel_id=1, replica_groups=mesh['section'=32,'neuron'=16] {'neuron'}, dimensions={1}, use_global_device_ids=true | all-gather | bytes 417792 | tf_op jit(solution)/shard_map/all_gather | solution.py:46
  461.1 16.4 %all_gather.117 = bf16[6,32768]{1,0:T(8,128)(2,1)S(1)} all-gather(bf16[6,2048]{1,0:T(8,128)(2,1)S(1)} %collective-permute-done.20), channel_id=1, replica_groups=mesh['section'=32,'neuron'=16] {'neuron'}, dimensions={1}, use_global_device_ids=true | all-gather | bytes 417792 | tf_op jit(solution)/shard_map/all_gather | solution.py:46
  482.6 16.7 %all_gather.118 = bf16[6,32768]{1,0:T(8,128)(2,1)S(1)} all-gather(bf16[6,2048]{1,0:T(8,128)(2,1)S(1)} %collective-permute-done.21), channel_id=1, replica_groups=mesh['section'=32,'neuron'=16] {'neuron'}, dimensions={1}, use_global_device_ids=true | all-gather | bytes 417792 | tf_op jit(solution)/shard_map/all_gather | solution.py:46
  504.4 16.4 %all_gather.119 = bf16[6,32768]{1,0:T(8,128)(2,1)S(1)} all-gather(bf16[6,2048]{1,0:T(8,128)(2,1)S(1)} %collective-permute-done.22), channel_id=1, replica_groups=mesh['section'=32,'neuron'=16] {'neuron'}, dimensions={1}, use_global_device_ids=true | all-gather | bytes 417792 | tf_op jit(solution)/shard_map/all_gather | solution.py:46
  525.9 16.9 %all_gather.120 = bf16[6,32768]{1,0:T(8,128)(2,1)S(1)} all-gather(bf16[6,2048]{1,0:T(8,128)(2,1)S(1)} %collective-permute-done.23), channel_id=1, replica_groups=mesh['section'=32,'neuron'=16] {'neuron'}, dimensions={1}, use_global_device_ids=true | all-gather | bytes 417792 | tf_op jit(solution)/shard_map/all_gather | solution.py:46
  547.8 16.4 %all_gather.121 = bf16[6,32768]{1,0:T(8,128)(2,1)S(1)} all-gather(bf16[6,2048]{1,0:T(8,128)(2,1)S(1)} %collective-permute-done.24), channel_id=1, replica_groups=mesh['section'=32,'neuron'=16] {'neuron'}, dimensions={1}, use_global_device_ids=true | all-gather | bytes 417792 | tf_op jit(solution)/shard_map/all_gather | solution.py:46
  569.3 16.7 %all_gather.122 = bf16[6,32768]{1,0:T(8,128)(2,1)S(1)} all-gather(bf16[6,2048]{1,0:T(8,128)(2,1)S(1)} %collective-permute-done.25), channel_id=1, replica_groups=mesh['section'=32,'neuron'=16] {'neuron'}, dimensions={1}, use_global_device_ids=true | all-gather | bytes 417792 | tf_op jit(solution)/shard_map/all_gather | solution.py:46
  591.1 16.4 %all_gather.123 = bf16[6,32768]{1,0:T(8,128)(2,1)S(1)} all-gather(bf16[6,2048]{1,0:T(8,128)(2,1)S(1)} %collective-permute-done.26), channel_id=1, replica_groups=mesh['section'=32,'neuron'=16] {'neuron'}, dimensions={1}, use_global_device_ids=true | all-gather | bytes 417792 | tf_op jit(solution)/shard_map/all_gather | solution.py:46
  612.6 16.7 %all_gather.124 = bf16[6,32768]{1,0:T(8,128)(2,1)S(1)} all-gather(bf16[6,2048]{1,0:T(8,128)(2,1)S(1)} %collective-permute-done.27), channel_id=1, replica_groups=mesh['section'=32,'neuron'=16] {'neuron'}, dimensions={1}, use_global_device_ids=true | all-gather | bytes 417792 | tf_op jit(solution)/shard_map/all_gather | solution.py:46
  634.3 16.5 %all_gather.125 = bf16[6,32768]{1,0:T(8,128)(2,1)S(1)} all-gather(bf16[6,2048]{1,0:T(8,128)(2,1)S(1)} %collective-permute-done.28), channel_id=1, replica_groups=mesh['section'=32,'neuron'=16] {'neuron'}, dimensions={1}, use_global_device_ids=true | all-gather | bytes 417792 | tf_op jit(solution)/shard_map/all_gather | solution.py:46
  655.9 16.7 %all_gather.126 = bf16[6,32768]{1,0:T(8,128)(2,1)S(1)} all-gather(bf16[6,2048]{1,0:T(8,128)(2,1)S(1)} %collective-permute-done.29), channel_id=1, replica_groups=mesh['section'=32,'neuron'=16] {'neuron'}, dimensions={1}, use_global_device_ids=true | all-gather | bytes 417792 | tf_op jit(solution)/shard_map/all_gather | solution.py:46
  679.2 107.5 %collective-permute-done.30 = bf16[6,2048]{1,0:T(8,128)(2,1)S(1)} collective-permute-done((bf16[6,2048]{1,0:T(8,128)(2,1)S(1)}, bf16[6,2048]{1,0:T(8,128)(2,1)S(1)}, u32[]{:S(2)}, u32[]{:S(2)}) %collective-permute-start.30) | collective-permute-done | bytes 24608 | tf_op jit(solution)/shard_map/ppermute | solution.py:52
  786.7 17.9 %all_gather.127 = bf16[6,32768]{1,0:T(8,128)(2,1)S(1)} all-gather(bf16[6,2048]{1,0:T(8,128)(2,1)S(1)} %collective-permute-done.30), channel_id=1, replica_groups=mesh['section'=32,'neuron'=16] {'neuron'}, dimensions={1}, use_global_device_ids=true | all-gather | bytes 417792 | tf_op jit(solution)/shard_map/all_gather | solution.py:46
  (224 shorter events, 312.4 us)
Async XLA Ops:
  25.5 0.7 collective-permute-start
  47.0 0.7 collective-permute-start.1
  69.0 0.7 collective-permute-start.2
  90.5 0.7 collective-permute-start.3
  112.5 0.7 collective-permute-start.4
  134.1 0.7 collective-permute-start.5
  156.0 0.7 collective-permute-start.6
  177.6 0.7 collective-permute-start.7
  200.0 0.7 collective-permute-start.8
  221.5 0.7 collective-permute-start.9
  243.5 0.7 collective-permute-start.10
  265.0 0.7 collective-permute-start.11
  330.5 0.7 collective-permute-start.14
  395.4 0.7 collective-permute-start.17
  438.7 0.7 collective-permute-start.19
  460.4 0.7 collective-permute-start.20
  481.9 0.7 collective-permute-start.21
  503.7 0.7 collective-permute-start.22
  525.2 0.7 collective-permute-start.23
  547.2 0.7 collective-permute-start.24
  590.4 0.7 collective-permute-start.26
  611.9 0.7 collective-permute-start.27
  655.2 0.7 collective-permute-start.29
  676.9 109.8 %collective-permute-start.30 = (bf16[6,2048]{1,0:T(8,128)(2,1)S(1)}, bf16[6,2048]{1,0:T(8,128)(2,1)S(1)}, u32[]{:S(2)}, u32[]{:S(2)}) collective-permute-start(bf16[6,2048]{1,0:T(8,128)(2,1)S(1)} %bitcast.647), channel_id=1, source_target_pairs={{480,496},{481,497},{482,498},{483,499},{484,500},{485,501},{486,5... | collective-permute-start | bytes 73736 | tf_op jit(solution)/shard_map/ppermute | solution.py:52
  (10 other events, 111.1 us)
where the time goes:
time: 820 us; the launch traced here: 810 us
  blocking collectives  536 us (65%)
  matrix products  117 us (14%)
  waiting for transfers between devices  108 us (13%)
  local copies, waits for them, and re-layouts  25.1 us (3%)
  starting transfers between devices  21.2 us (3%)
    all_gather x32, blocking collectives, step(): gathered = lax.all_gather(current, 'neuron', axis=1, tiled=True)  536 us
    dot_general x32, matrix products, layer_apply(): jnp.einsum('msk,skj->msj', picked, weight_tiles[0], preferred_element_typ...  108 us
    ppermute x31, waiting for transfers between devices, step(): return (lax.ppermute(result, 'section', route), collected)  108 us
    gather x32, local copies, waits for them, and re-layouts, layer_apply(): picked = shaped.at[:, source].get(mode='promise_in_bounds')  23.9 us
    ppermute x31, starting transfers between devices, step(): return (lax.ppermute(result, 'section', route), collected)  21.2 us
  transfers between devices with their start and end apart: 31, of which 1 were waited for; matrix products, arithmetic and copies ran while one was open for 0% of the time, Pallas kernels for 0%

commit v1 on v0

--- a/solution.py
+++ b/solution.py
@@ -43,7 +43,10 @@
         return jnp.zeros((row_count, shard_width), jnp.bfloat16)
 
     def step(step_num, current, collected, route):
-        gathered = lax.all_gather(current, "neuron", axis=1, tiled=True)
+        formed = jnp.concatenate([current for _ in range(jax.lax.axis_size("neuron"))], axis=1)
+        gathered = jax.lax.all_to_all(
+            formed, axis_name="neuron", tiled=True, split_axis=1, concat_axis=1
+        )
         active = section_pos == step_num
         result = compute(gathered)
         collected = jnp.where(active, result, collected)

time: 820 us -> 1260 us (1.54)
  local copies, waits for them, and re-layouts: 25.1 us -> 349 us
  blocking collectives: 536 us -> 586 us
  waiting for transfers between devices: 108 us -> 157 us
  starting transfers between devices: 21.2 us -> 36.5 us
    all_to_all x0 -> x29, blocking collectives: none -> 586 us  [step(): jax.lax.all_to_all(formed, axis_name='neuron', tiled=True, split_axis=1,...]
    all_gather x32 -> x0, blocking collectives: 536 us -> none  [step(): gathered = lax.all_gather(current, 'neuron', axis=1, tiled=True)]
    unnamed x37 -> x515, local copies, waits for them, and re-layouts: 0.37 us -> 302 us
    all_to_all x0 -> x3, waiting for transfers between devices: none -> 48.8 us  [step(): jax.lax.all_to_all(formed, axis_name='neuron', tiled=True, split_axis=1,...]
    concatenate x0 -> x32, local copies, waits for them, and re-layouts: none -> 20.2 us  [step(): jnp.concatenate([current for _ in range(jax.lax.axis_size('neuron'))], ax...]
    all_to_all x0 -> x3, starting transfers between devices: none -> 15.3 us  [step(): jax.lax.all_to_all(formed, axis_name='neuron', tiled=True, split_axis=1,...]
  transfers between devices with their start and end apart: 31 -> 34, of which waited for: 1 -> 4; matrix products, arithmetic and copies ran while one was open for 0% -> 0% of each run, Pallas kernels for 0% -> 0%
where the time goes in v1:
time: 1260 us; the launch traced here: 1250 us
  blocking collectives  586 us (47%)
  local copies, waits for them, and re-layouts  349 us (28%)
  waiting for transfers between devices  157 us (12%)
  matrix products  117 us (9%)
  starting transfers between devices  36.5 us (3%)
    all_to_all x29, blocking collectives, step(): jax.lax.all_to_all(formed, axis_name='neuron', tiled=True, split_axis=1,...  586 us
    unnamed x515, local copies, waits for them, and re-layouts  302 us
    ppermute x31, waiting for transfers between devices, step(): return (lax.ppermute(result, 'section', route), collected)  109 us
    dot_general x32, matrix products, layer_apply(): jnp.einsum('msk,skj->msj', picked, weight_tiles[0], preferred_element_typ...  108 us
    all_to_all x3, waiting for transfers between devices, step(): jax.lax.all_to_all(formed, axis_name='neuron', tiled=True, split_axis=1,...  48.8 us
    gather x32, local copies, waits for them, and re-layouts, layer_apply(): picked = shaped.at[:, source].get(mode='promise_in_bounds')  25.9 us
  transfers between devices with their start and end apart: 34, of which 4 were waited for; matrix products, arithmetic and copies ran while one was open for 0% of the time, Pallas kernels for 0%

profile of v1, /device:TPU:455, one launch (start us, length us, event | category | flops | bytes accessed | tf_op | source)
XLA Modules:
  0.0 1249.8 jit_solution(4483261639326516877)
XLA Ops:
  96.6 20.2 %all_to_all.289 = bf16[6,16,2048]{2,0,1:T(8,128)(2,1)S(1)} all-to-all(bf16[6,16,2048]{2,0,1:T(8,128)(2,1)} %bitcast.632), channel_id=1, replica_groups=mesh['section'=32,'neuron'=16] {'neuron'}, dimensions={1} | all-to-all | bytes 786432 | tf_op jit(solution)/shard_map/all_to_all | solution.py:47
  131.7 20.2 %all_to_all.290 = bf16[6,16,2048]{2,0,1:T(8,128)(2,1)S(1)} all-to-all(bf16[6,16,2048]{2,0,1:T(8,128)(2,1)} %bitcast.633), channel_id=1, replica_groups=mesh['section'=32,'neuron'=16] {'neuron'}, dimensions={1} | all-to-all | bytes 786432 | tf_op jit(solution)/shard_map/all_to_all | solution.py:47
  166.7 20.2 %all_to_all.291 = bf16[6,16,2048]{2,0,1:T(8,128)(2,1)S(1)} all-to-all(bf16[6,16,2048]{2,0,1:T(8,128)(2,1)} %bitcast.634), channel_id=1, replica_groups=mesh['section'=32,'neuron'=16] {'neuron'}, dimensions={1} | all-to-all | bytes 786432 | tf_op jit(solution)/shard_map/all_to_all | solution.py:47
  201.8 20.2 %all_to_all.292 = bf16[6,16,2048]{2,0,1:T(8,128)(2,1)S(1)} all-to-all(bf16[6,16,2048]{2,0,1:T(8,128)(2,1)} %bitcast.635), channel_id=1, replica_groups=mesh['section'=32,'neuron'=16] {'neuron'}, dimensions={1} | all-to-all | bytes 786432 | tf_op jit(solution)/shard_map/all_to_all | solution.py:47
  236.8 20.2 %all_to_all.293 = bf16[6,16,2048]{2,0,1:T(8,128)(2,1)S(1)} all-to-all(bf16[6,16,2048]{2,0,1:T(8,128)(2,1)} %bitcast.636), channel_id=1, replica_groups=mesh['section'=32,'neuron'=16] {'neuron'}, dimensions={1} | all-to-all | bytes 786432 | tf_op jit(solution)/shard_map/all_to_all | solution.py:47
  271.9 20.3 %all_to_all.294 = bf16[6,16,2048]{2,0,1:T(8,128)(2,1)S(1)} all-to-all(bf16[6,16,2048]{2,0,1:T(8,128)(2,1)} %bitcast.637), channel_id=1, replica_groups=mesh['section'=32,'neuron'=16] {'neuron'}, dimensions={1} | all-to-all | bytes 786432 | tf_op jit(solution)/shard_map/all_to_all | solution.py:47
  307.1 20.2 %all_to_all.295 = bf16[6,16,2048]{2,0,1:T(8,128)(2,1)S(1)} all-to-all(bf16[6,16,2048]{2,0,1:T(8,128)(2,1)} %bitcast.638), channel_id=1, replica_groups=mesh['section'=32,'neuron'=16] {'neuron'}, dimensions={1} | all-to-all | bytes 786432 | tf_op jit(solution)/shard_map/all_to_all | solution.py:47
  342.2 20.2 %all_to_all.296 = bf16[6,16,2048]{2,0,1:T(8,128)(2,1)S(1)} all-to-all(bf16[6,16,2048]{2,0,1:T(8,128)(2,1)} %bitcast.639), channel_id=1, replica_groups=mesh['section'=32,'neuron'=16] {'neuron'}, dimensions={1} | all-to-all | bytes 786432 | tf_op jit(solution)/shard_map/all_to_all | solution.py:47
  377.2 20.2 %all_to_all.297 = bf16[6,16,2048]{2,0,1:T(8,128)(2,1)S(1)} all-to-all(bf16[6,16,2048]{2,0,1:T(8,128)(2,1)} %bitcast.640), channel_id=1, replica_groups=mesh['section'=32,'neuron'=16] {'neuron'}, dimensions={1} | all-to-all | bytes 786432 | tf_op jit(solution)/shard_map/all_to_all | solution.py:47
  412.3 20.2 %all_to_all.298 = bf16[6,16,2048]{2,0,1:T(8,128)(2,1)S(1)} all-to-all(bf16[6,16,2048]{2,0,1:T(8,128)(2,1)} %bitcast.641), channel_id=1, replica_groups=mesh['section'=32,'neuron'=16] {'neuron'}, dimensions={1} | all-to-all | bytes 786432 | tf_op jit(solution)/shard_map/all_to_all | solution.py:47
  447.3 20.2 %all_to_all.299 = bf16[6,16,2048]{2,0,1:T(8,128)(2,1)S(1)} all-to-all(bf16[6,16,2048]{2,0,1:T(8,128)(2,1)} %bitcast.642), channel_id=1, replica_groups=mesh['section'=32,'neuron'=16] {'neuron'}, dimensions={1} | all-to-all | bytes 786432 | tf_op jit(solution)/shard_map/all_to_all | solution.py:47
  482.4 20.2 %all_to_all.300 = bf16[6,16,2048]{2,0,1:T(8,128)(2,1)S(1)} all-to-all(bf16[6,16,2048]{2,0,1:T(8,128)(2,1)} %bitcast.643), channel_id=1, replica_groups=mesh['section'=32,'neuron'=16] {'neuron'}, dimensions={1} | all-to-all | bytes 786432 | tf_op jit(solution)/shard_map/all_to_all | solution.py:47
  517.5 20.2 %all_to_all.301 = bf16[6,16,2048]{2,0,1:T(8,128)(2,1)S(1)} all-to-all(bf16[6,16,2048]{2,0,1:T(8,128)(2,1)} %bitcast.644), channel_id=1, replica_groups=mesh['section'=32,'neuron'=16] {'neuron'}, dimensions={1} | all-to-all | bytes 786432 | tf_op jit(solution)/shard_map/all_to_all | solution.py:47
  587.8 20.2 %all_to_all.302 = bf16[6,16,2048]{2,0,1:T(8,128)(2,1)S(1)} all-to-all(bf16[6,16,2048]{2,0,1:T(8,128)(2,1)} %bitcast.646), channel_id=1, replica_groups=mesh['section'=32,'neuron'=16] {'neuron'}, dimensions={1} | all-to-all | bytes 786432 | tf_op jit(solution)/shard_map/all_to_all | solution.py:47
  622.8 20.2 %all_to_all.303 = bf16[6,16,2048]{2,0,1:T(8,128)(2,1)S(1)} all-to-all(bf16[6,16,2048]{2,0,1:T(8,128)(2,1)} %bitcast.647), channel_id=1, replica_groups=mesh['section'=32,'neuron'=16] {'neuron'}, dimensions={1} | all-to-all | bytes 786432 | tf_op jit(solution)/shard_map/all_to_all | solution.py:47
  657.9 20.2 %all_to_all.304 = bf16[6,16,2048]{2,0,1:T(8,128)(2,1)S(1)} all-to-all(bf16[6,16,2048]{2,0,1:T(8,128)(2,1)} %bitcast.648), channel_id=1, replica_groups=mesh['section'=32,'neuron'=16] {'neuron'}, dimensions={1} | all-to-all | bytes 786432 | tf_op jit(solution)/shard_map/all_to_all | solution.py:47
  693.0 20.2 %all_to_all.305 = bf16[6,16,2048]{2,0,1:T(8,128)(2,1)S(1)} all-to-all(bf16[6,16,2048]{2,0,1:T(8,128)(2,1)} %bitcast.649), channel_id=1, replica_groups=mesh['section'=32,'neuron'=16] {'neuron'}, dimensions={1} | all-to-all | bytes 786432 | tf_op jit(solution)/shard_map/all_to_all | solution.py:47
  728.0 20.2 %all_to_all.306 = bf16[6,16,2048]{2,0,1:T(8,128)(2,1)S(1)} all-to-all(bf16[6,16,2048]{2,0,1:T(8,128)(2,1)} %bitcast.650), channel_id=1, replica_groups=mesh['section'=32,'neuron'=16] {'neuron'}, dimensions={1} | all-to-all | bytes 786432 | tf_op jit(solution)/shard_map/all_to_all | solution.py:47
  763.1 20.2 %all_to_all.307 = bf16[6,16,2048]{2,0,1:T(8,128)(2,1)S(1)} all-to-all(bf16[6,16,2048]{2,0,1:T(8,128)(2,1)} %bitcast.651), channel_id=1, replica_groups=mesh['section'=32,'neuron'=16] {'neuron'}, dimensions={1} | all-to-all | bytes 786432 | tf_op jit(solution)/shard_map/all_to_all | solution.py:47
  798.1 20.6 %all_to_all.308 = bf16[6,16,2048]{2,0,1:T(8,128)(2,1)S(1)} all-to-all(bf16[6,16,2048]{2,0,1:T(8,128)(2,1)} %bitcast.652), channel_id=1, replica_groups=mesh['section'=32,'neuron'=16] {'neuron'}, dimensions={1} | all-to-all | bytes 786432 | tf_op jit(solution)/shard_map/all_to_all | solution.py:47
  833.6 20.2 %all_to_all.309 = bf16[6,16,2048]{2,0,1:T(8,128)(2,1)S(1)} all-to-all(bf16[6,16,2048]{2,0,1:T(8,128)(2,1)} %bitcast.653), channel_id=1, replica_groups=mesh['section'=32,'neuron'=16] {'neuron'}, dimensions={1} | all-to-all | bytes 786432 | tf_op jit(solution)/shard_map/all_to_all | solution.py:47
  903.7 20.2 %all_to_all.311 = bf16[6,16,2048]{2,0,1:T(8,128)(2,1)S(1)} all-to-all(bf16[6,16,2048]{2,0,1:T(8,128)(2,1)} %bitcast.655), channel_id=1, replica_groups=mesh['section'=32,'neuron'=16] {'neuron'}, dimensions={1} | all-to-all | bytes 786432 | tf_op jit(solution)/shard_map/all_to_all | solution.py:47
  1079.0 20.4 %all_to_all.316 = bf16[6,16,2048]{2,0,1:T(8,128)(2,1)S(1)} all-to-all(bf16[6,16,2048]{2,0,1:T(8,128)(2,1)} %bitcast.660), channel_id=1, replica_groups=mesh['section'=32,'neuron'=16] {'neuron'}, dimensions={1} | all-to-all | bytes 786432 | tf_op jit(solution)/shard_map/all_to_all | solution.py:47
  1105.1 108.5 %collective-permute-done.30 = bf16[6,2048]{1,0:T(8,128)(2,1)S(1)} collective-permute-done((bf16[6,2048]{1,0:T(8,128)(2,1)S(1)}, bf16[6,2048]{1,0:T(8,128)(2,1)S(1)}, u32[]{:S(2)}, u32[]{:S(2)}) %collective-permute-start.30) | collective-permute-done | bytes 24608 | tf_op jit(solution)/shard_map/ppermute | solution.py:55
  (737 shorter events, 674.3 us)
Async XLA Ops:
  21.8 25.0 %all-to-all-start = ((bf16[6,16,2048]{2,0,1:T(8,128)(2,1)}), bf16[6,16,2048]{2,0,1:T(8,128)(2,1)S(1)}, u32[]{:S(2)}, u32[]{:S(2)}) async-start(bf16[6,16,2048]{2,0,1:T(8,128)(2,1)} %bitcast.3), calls=%async_computation | async-start | bytes 1048576 | tf_op jit(solution)/shard_map/all_to_all | solution.py:47
  51.2 0.7 collective-permute-start
  86.2 0.7 collective-permute-start.1
  121.3 0.7 collective-permute-start.2
  156.3 0.7 collective-permute-start.3
  191.4 0.7 collective-permute-start.4
  226.5 0.7 collective-permute-start.5
  261.5 0.7 collective-permute-start.6
  296.7 0.7 collective-permute-start.7
  331.8 0.7 collective-permute-start.8
  366.8 0.7 collective-permute-start.9
  401.9 0.7 collective-permute-start.10
  437.0 0.7 collective-permute-start.11
  472.0 0.7 collective-permute-start.12
  507.1 0.7 collective-permute-start.13
  542.1 0.7 collective-permute-start.14
  552.5 20.4 %all-to-all-start.15 = ((bf16[6,16,2048]{2,0,1:T(8,128)(2,1)}), bf16[6,16,2048]{2,0,1:T(8,128)(2,1)S(1)}, u32[]{:S(2)}, u32[]{:S(2)}) async-start(bf16[6,16,2048]{2,0,1:T(8,128)(2,1)} %bitcast.645), calls=%async_computation.15 | async-start | bytes 1048576 | tf_op jit(solution)/shard_map/all_to_all | solution.py:47
  577.4 0.7 collective-permute-start.15
  612.5 0.7 collective-permute-start.16
  647.5 0.7 collective-permute-start.17
  787.8 0.7 collective-permute-start.21
  893.3 0.7 collective-permute-start.24
  1103.8 109.8 %collective-permute-start.30 = (bf16[6,2048]{1,0:T(8,128)(2,1)S(1)}, bf16[6,2048]{1,0:T(8,128)(2,1)S(1)}, u32[]{:S(2)}, u32[]{:S(2)}) collective-permute-start(bf16[6,2048]{1,0:T(8,128)(2,1)S(1)} %bitcast.770), channel_id=1, source_target_pairs={{480,496},{481,497},{482,498},{483,499},{484,500},{485,501},{486,5... | collective-permute-start | bytes 73736 | tf_op jit(solution)/shard_map/ppermute | solution.py:55
  1223.3 21.1 %all-to-all-start.31 = ((bf16[6,16,2048]{2,0,1:T(8,128)(2,1)}), bf16[6,16,2048]{2,0,1:T(8,128)(2,1)S(1)}, u32[]{:S(2)}, u32[]{:S(2)}) async-start(bf16[6,16,2048]{2,0,1:T(8,128)(2,1)} %bitcast.661), calls=%async_computation.31 | async-start | bytes 1048576 | tf_op jit(solution)/shard_map/all_to_all | solution.py:47
  (12 other events, 108.4 us)
